TPU v7x, 256 devices: a whole 4x4x8 slice. The times are simulated.
256 devices in a mesh: blk: 64 (over z_hi, x, y, core), path: 4 (over z_lo).
Axes of the slice: x: 4, y: 4, z: 8 (z_hi: 2, z_lo: 4; z = z_hi * 4 + z_lo), core: 2. Of those that a mesh axis runs over, the one named last changes fastest.
Arguments:
- records: bfloat16 [65536, 512], P('blk'), may hold values from -87.98545 to 87.98545
- coefficients: float32 [65536, 64], P('blk', 'path'), may hold values from -6 to 6
- velocity: float32 [65536, 64], P('blk', 'path'), may hold values from -3 to 3
- targets: float32 [65536, 64], P('blk', 'path'), may hold values from -6 to 6
- block_local: int32 [3, 1536], P(None, 'blk'), may hold values from 0 to 1023
- block_count: int32 [3, 64], replicated, may hold values from 1 to 24, 1024 in all within a row
- candidates: bfloat16 [32768, 512], P('blk'), may hold values from -87.98545 to 87.98545
- frequencies: bfloat16 [512, 1024], replicated, may hold values from -0.25 to 0.25
- phases: float32 [1024], replicated, may hold values from -3.140625 to 3.140625
- prior_weight: float32 [1024, 64], P(None, 'path'), may hold values from -6 to 6
Outputs:
- coefficients_out: float32 [65536, 64], P('blk', 'path')
- velocity_out: float32 [65536, 64], P('blk', 'path')
- scores: float32 [32768, 64], P('blk', 'path')
- path_rms: float32 [32768], P('blk')
Inputs may be any that keep to these rules, and one draw needn't show every extreme that they name: `block_count`: each row sums to 1024, and its largest entry is exactly 24. `block_local`: index within the owner's records; a slot at or beyond the owner's count in that step is not used. Used entries of one owner may repeat.
All inputs are finite; a program needn't handle non-finite values.
Results may differ from a plain program's by a relative error of at most 0.0014.
Values may be sent and summed in bfloat16 or wider, within the bound.
No kernel may reach another device: no remote copies, remote signals or barrier semaphores. Data moves between devices by JAX's collectives and lax.ppermute only.
A program may use at most 128 MiB of HBM per device.

v0:
```python
import math
import jax
import jax.numpy as jnp
from jax import lax
from jax.sharding import PartitionSpec as P

NOISE = 0.5
MOMENTUM = 0.9
RATE = 0.3
EPSILON = 1e-06
SIGNAL = 9.0


def passed_along(shard, axis, by):
    length = lax.axis_size(axis)
    return lax.ppermute(shard, axis, [(i, (i + by) % length) for i in range(length)])


def square_norms(row_block):
    widened = row_block.astype(jnp.float32)
    return jnp.sum(widened * widened, axis=1)


def kernel_apply(left_rows, left_norms, right_rows, right_norms, weights):
    dot_values = lax.dot_general(
        left_rows, right_rows, (((1,), (1,)), ((), ())), preferred_element_type=jnp.float32
    )
    distance = left_norms[:, None] + right_norms[None, :] - 2.0 * dot_values
    kernel_tile = SIGNAL * jnp.exp(-distance / left_rows.shape[1])
    return jnp.dot(kernel_tile, weights, precision=lax.Precision.HIGHEST)


def prior_values(cand_rows, frequencies, phases, prior_weight):
    angles = (
        jnp.dot(cand_rows, frequencies, preferred_element_type=jnp.float32) * math.sqrt(2.0)
        + phases[None, :]
    )
    features = math.sqrt(2.0 * SIGNAL / frequencies.shape[1]) * jnp.cos(angles)
    return jnp.dot(features, prior_weight, precision=lax.Precision.HIGHEST)


def shards(
    records,
    coefficients,
    velocity,
    targets,
    block_local,
    block_count,
    candidates,
    frequencies,
    phases,
    prior_weight,
):
    record_total = records.shape[0] * lax.axis_size("blk")
    root_count = jnp.sqrt(jnp.float32(record_total))
    slot_count = block_local.shape[1]
    own_index = lax.axis_index("blk")
    neighbour = passed_along(candidates, "blk", 1)
    work_norms = square_norms(records)
    slot_ids = jnp.arange(slot_count, dtype=jnp.int32)
    for repeat in range(block_local.shape[0]):
        local_rows = block_local[repeat]
        own_count = lax.dynamic_index_in_dim(block_count[repeat], own_index, 0, keepdims=False)
        is_live = slot_ids < own_count
        gathered = lax.all_gather(records[local_rows], "blk", axis=0, tiled=True)
        gathered_norms = square_norms(gathered)
        work_coefs = coefficients
        whole_sum = lax.psum(
            kernel_apply(gathered, gathered_norms, records, work_norms, work_coefs), "blk"
        )
        product = lax.dynamic_slice_in_dim(whole_sum, own_index * slot_count, slot_count, 0)
        product = product / root_count
        gradient = jnp.where(
            is_live[:, None], product + NOISE * coefficients[local_rows] - targets[local_rows], 0.0
        )
        velocity = (MOMENTUM * velocity).at[local_rows].add(-RATE * gradient)
        coefficients = coefficients + velocity
    own_sum = kernel_apply(candidates, square_norms(candidates), records, work_norms, coefficients)
    next_sum = kernel_apply(neighbour, square_norms(neighbour), records, work_norms, coefficients)
    own_sum, next_sum = (own_sum, next_sum)
    first_part = prior_values(candidates, frequencies, phases, prior_weight) + own_sum / root_count
    next_term = next_sum / root_count
    passed = passed_along(first_part, "blk", 1)
    scores = passed_along(passed + next_term, "blk", 1)
    squares_local = jnp.sum(scores * scores, axis=1)
    summed = lax.psum(squares_local, "path")
    path_rms = jnp.sqrt(summed / (scores.shape[1] * lax.axis_size("path")) + EPSILON)
    return (coefficients, velocity, scores, path_rms)


def solution(mesh):
    return jax.shard_map(
        shards,
        mesh=mesh,
        in_specs=(
            P("blk", None),
            P("blk", "path"),
            P("blk", "path"),
            P("blk", "path"),
            P(None, "blk"),
            P(),
            P("blk", None),
            P(),
            P(),
            P(None, "path"),
        ),
        out_specs=(P("blk", "path"), P("blk", "path"), P("blk", "path"), P("blk")),
        check_vma=False,
    )
```

profile of v0, /device:TPU:0, one launch (start us, length us, event | category | flops | bytes accessed | tf_op | source)
XLA Modules:
  0.0 2484.4 jit_solution(10862809576927528547)
XLA Ops:
  7.3 0.9 fusion.87
  8.2 2.6 gather_fusion
  10.8 2.6 gather_fusion.3
  13.5 2.6 gather_fusion.6
  16.2 1.0 copy.32
  19.1 1.0 copy.36
  20.8 1.0 copy.34
  22.5 0.7 constant_dynamic-slice_fusion
  23.2 0.6 iota_compare_fusion.2
  23.8 0.6 iota_compare_fusion.1
  24.5 0.6 iota_compare_fusion
  25.6 2.1 fusion.110
  27.7 2.0 fusion.109
  29.7 64.4 %all-gather.7.cloned.1.call-done = bf16[1536,512]{1,0:T(8,128)(2,1)} async-done(((bf16[24,512]{1,0:T(8,128)(2,1)}), bf16[1536,512]{1,0:T(8,128)(2,1)}) %all-gather.7.cloned.1.call-update) | async-done | bytes 1572880 | tf_op jit(solution)/shard_map/all_gather | solution.py:65
  94.1 1.8 multiply_reduce_fusion.2
  95.9 3.3 fusion.106
  99.2 7.4 fusion.16
  107.0 65.2 %all-gather.9.cloned.1.call-done = bf16[1536,512]{1,0:T(8,128)(2,1)} async-done(((bf16[24,512]{1,0:T(8,128)(2,1)}), bf16[1536,512]{1,0:T(8,128)(2,1)}) %all-gather.9.cloned.1.call-update) | async-done | bytes 1572880 | tf_op jit(solution)/shard_map/all_gather | solution.py:65
  172.2 5.9 fusion.107
  178.1 72.2 %all-gather.11.cloned.1.call-done = bf16[1536,512]{1,0:T(8,128)(2,1)} async-done(((bf16[24,512]{1,0:T(8,128)(2,1)}), bf16[1536,512]{1,0:T(8,128)(2,1)}) %all-gather.11.cloned.1.call-update) | async-done | bytes 1572880 | tf_op jit(solution)/shard_map/all_gather | solution.py:65
  250.3 6.0 fusion.108
  256.7 707.5 %all-reduce.4.cloned.1.call-done = f32[1536,16]{0,1:T(8,128)} async-done(((f32[1536,16]{0,1:T(8,128)}), f32[1536,16]{0,1:T(8,128)}) %all-reduce.4.cloned.1.call-update) | async-done | bytes 98320 | tf_op jit(solution)/shard_map/psum | solution.py:68
  964.2 0.8 select_multiply_fusion.2
  965.1 0.9 scatter_fusion
  966.0 0.9 broadcast_multiply_fusion
  966.9 0.8 copy-done.5
  967.7 10.3 fusion.8
  978.1 1.8 multiply_reduce_fusion
  979.9 1.6 gather_fusion.4
  981.5 711.6 %all-reduce.6.cloned.1.call-done = f32[1536,16]{0,1:T(8,128)} async-done(((f32[1536,16]{0,1:T(8,128)}), f32[1536,16]{0,1:T(8,128)}) %all-reduce.6.cloned.1.call-update) | async-done | bytes 98320 | tf_op jit(solution)/shard_map/psum | solution.py:68
  1693.2 0.8 select_multiply_fusion.1
  1694.0 3.0 scatter_fusion.1
  1697.0 1.3 broadcast_multiply_fusion.1
  1698.3 10.2 fusion
  1708.5 3.1 fusion.111
  1712.3 711.4 %all-reduce.8.cloned.1.call-done = f32[1536,16]{0,1:T(8,128)} async-done(((f32[1536,16]{0,1:T(8,128)}), f32[1536,16]{0,1:T(8,128)}) %all-reduce.8.cloned.1.call-update) | async-done | bytes 98320 | tf_op jit(solution)/shard_map/psum | solution.py:68
  2423.7 0.8 select_multiply_fusion
  2424.6 0.9 scatter_fusion.2
  2425.6 4.1 fusion.63
  2429.7 9.1 fusion.60
  2439.2 1.2 multiply_reduce_fusion.4
  2440.4 10.3 collective-permute-done
  2450.7 2.4 fusion.69
  2453.2 0.8 copy.45
  2454.0 0.8 copy.46
  2454.8 9.9 collective-permute-done.2
  2464.7 11.5 psum.31
  2476.8 0.6 copy.54
  (67 shorter events, 6.7 us)
Async XLA Ops:
  7.2 20.5 copy-start
  7.2 18.1 copy-start.1
  7.2 17.9 copy-start.3
  7.2 13.6 copy-start.10
  7.2 14.7 copy-start.12
  7.2 86.9 %all-gather.7.cloned.1.call-start = ((), (), s32[]{:S(2)}) async-start(), calls=%async_computation.3 | async-start | bytes 1597440 | tf_op jit(solution)/shard_map/all_gather | solution.py:65
  10.8 161.4 %all-gather.9.cloned.1.call-start = ((), (), s32[]{:S(2)}) async-start(), calls=%async_computation.4 | async-start | bytes 1597440 | tf_op jit(solution)/shard_map/all_gather | solution.py:65
  13.4 236.9 %all-gather.11.cloned.1.call-start = ((), (), s32[]{:S(2)}) async-start(), calls=%async_computation.5 | async-start | bytes 1597440 | tf_op jit(solution)/shard_map/all_gather | solution.py:65
  16.1 948.1 %all-reduce.4.cloned.1.call-start = ((), (), s32[]{:S(2)}) async-start(), calls=%async_computation | async-start | bytes 196608 | tf_op jit(solution)/shard_map/psum | solution.py:68
  16.1 1692.4 %collective-permute-start.1 = (bf16[512,512]{1,0:T(8,128)(2,1)}, bf16[512,512]{1,0:T(8,128)(2,1)}, u32[]{:S(2)}, u32[]{:S(2)}) collective-permute-start(bf16[512,512]{1,0:T(8,128)(2,1)} %param.16), channel_id=1, source_target_pairs={{0,4},{4,8},{8,12},{12,16},{16,20},{20,24},{24,28},{28,32},{32,36}... | collective-permute-start | bytes 1572872 | tf_op jit(solution)/shard_map/ppermute | solution.py:16
  95.9 3.3 copy-start.8
  106.7 1586.5 %all-reduce.6.cloned.1.call-start = ((), (), s32[]{:S(2)}) async-start(), calls=%async_computation.1 | async-start | bytes 196608 | tf_op jit(solution)/shard_map/psum | solution.py:68
  178.1 787.0 %copy-start.4 = (f32[1024,16]{1,0:T(8,128)S(1)}, f32[1024,16]{1,0:T(8,128)}, u32[]{:S(2)}) copy-start(f32[1024,16]{1,0:T(8,128)} %copy.34) | copy-start | bytes 196612
  250.3 6.0 copy-start.7
  966.9 0.8 copy-start.5
  978.0 1445.7 %all-reduce.8.cloned.1.call-start = ((), (), s32[]{:S(2)}) async-start(), calls=%async_computation.2 | async-start | bytes 196608 | tf_op jit(solution)/shard_map/psum | solution.py:68
  2425.5 4.2 copy-start.2
  2425.5 4.2 copy-start.9
  2425.6 4.2 copy-start.11
  2429.7 21.0 copy-start.6
  2438.9 11.8 collective-permute-start
  2453.1 11.6 collective-permute-start.2
Sparse Core Ops, SparseCore 0:
  12.2 81.8 all-gather.6
  98.3 73.8 all-gather.8
  176.4 73.8 all-gather.10
  252.8 711.4 all-reduce.3
  978.1 714.9 all-reduce.5
  1708.7 714.9 all-reduce.7
where the time goes:
time: 2490 us; the launch traced here: 2480 us
  waiting for transfers between devices  2350 us (94%)
  matrix products  66.2 us (3%)
    psum x3, waiting for transfers between devices, shards(): lax.psum(kernel_apply(gathered, gathered_norms, records, work_norms, work...  2130 us
    all_gather x3, waiting for transfers between devices, shards(): gathered = lax.all_gather(records[local_rows], 'blk', axis=0, tiled=True)  202 us
  transfers between devices with their start and end apart: 9, of which 8 were waited for; matrix products, arithmetic and copies ran while one was open for 3% of the time, Pallas kernels for 0%

commit v1 on v0

--- a/solution.py
+++ b/solution.py
@@ -3,12 +3,16 @@
 import jax.numpy as jnp
 from jax import lax
 from jax.sharding import PartitionSpec as P
+from jax.lax import all_to_all, axis_size
 
 NOISE = 0.5
 MOMENTUM = 0.9
 RATE = 0.3
 EPSILON = 1e-06
 SIGNAL = 9.0
+drive_screen = lambda local_block: jnp.concatenate(
+    all_to_all(jnp.stack([local_block for _ in range(axis_size("blk"))]), "blk", 0, 0), axis=0
+)
 
 
 def passed_along(shard, axis, by):
@@ -62,7 +66,7 @@
         local_rows = block_local[repeat]
         own_count = lax.dynamic_index_in_dim(block_count[repeat], own_index, 0, keepdims=False)
         is_live = slot_ids < own_count
-        gathered = lax.all_gather(records[local_rows], "blk", axis=0, tiled=True)
+        gathered = drive_screen(records[local_rows])
         gathered_norms = square_norms(gathered)
         work_coefs = coefficients
         whole_sum = lax.psum(

time: 2490 us -> 2400 us (0.964)
  waiting for transfers between devices: 2350 us -> 2230 us
  starting transfers between devices: 0.92 us -> 30.7 us
    all_gather x3 -> x0, waiting for transfers between devices: 202 us -> none  [shards(): gathered = lax.all_gather(records[local_rows], 'blk', axis=0, tiled=True)]
    all_to_all x0 -> x3, waiting for transfers between devices: none -> 86.5 us  [all_to_all(jnp.stack([local_block for _ in range(axis_size('blk'))]), 'bl...]
    all_to_all x0 -> x3, starting transfers between devices: none -> 29.3 us  [all_to_all(jnp.stack([local_block for _ in range(axis_size('blk'))]), 'bl...]
where the time goes in v1:
time: 2400 us; the launch traced here: 2390 us
  waiting for transfers between devices  2230 us (93%)
  matrix products  66.1 us (3%)
  starting transfers between devices  30.7 us (1%)
    psum x3, waiting for transfers between devices, shards(): lax.psum(kernel_apply(gathered, gathered_norms, records, work_norms, work...  2120 us
    all_to_all x3, waiting for transfers between devices, all_to_all(jnp.stack([local_block for _ in range(axis_size('blk'))]), 'bl...  86.5 us
  transfers between devices with their start and end apart: 9, of which 8 were waited for; matrix products, arithmetic and copies ran while one was open for 3% of the time, Pallas kernels for 0%

profile of v1, /device:TPU:0, one launch (start us, length us, event | category | flops | bytes accessed | tf_op | source)
XLA Modules:
  0.0 2391.2 jit_solution(8808489701617389511)
XLA Ops:
  7.2 0.8 fusion.87
  8.0 2.0 gather_fusion
  10.0 1.2 stack.6
  11.2 13.1 all-to-all-start
  25.0 38.5 %all-to-all-done = bf16[64,24,512]{2,1,0:T(8,128)(2,1)} async-done(((bf16[64,24,512]{2,1,0:T(8,128)(2,1)}), bf16[64,24,512]{2,1,0:T(8,128)(2,1)}, u32[]{:S(2)}, u32[]{:S(2)}) %all-to-all-start) | async-done | bytes 1572896 | tf_op jit(solution)/shard_map/all_to_all | solution.py:14
  63.5 1.2 stack.7
  64.7 8.2 all-to-all-start.1
  76.5 1.0 copy.52
  77.7 35.2 %all-to-all-done.1 = bf16[64,24,512]{2,1,0:T(8,128)(2,1)} async-done(((bf16[64,24,512]{2,1,0:T(8,128)(2,1)}), bf16[64,24,512]{2,1,0:T(8,128)(2,1)}, u32[]{:S(2)}, u32[]{:S(2)}) %all-to-all-start.1) | async-done | bytes 1572896 | tf_op jit(solution)/shard_map/all_to_all | solution.py:14
  112.9 1.2 stack.8
  114.1 8.0 all-to-all-start.2
  124.4 0.7 iota_compare_fusion.1
  126.1 2.1 fusion.110
  128.2 2.0 fusion.109
  130.3 1.8 multiply_reduce_fusion.2
  132.2 3.3 fusion.106
  135.5 7.4 fusion.16
  143.5 5.9 fusion.107
  149.4 12.8 all-to-all-done.2
  162.2 5.9 fusion.108
  168.1 1.8 multiply_reduce_fusion.1
  169.9 698.1 %all-reduce.4.cloned.1.call-done = f32[1536,16]{0,1:T(8,128)} async-done(((f32[1536,16]{0,1:T(8,128)}), f32[1536,16]{0,1:T(8,128)}) %all-reduce.4.cloned.1.call-update) | async-done | bytes 98320 | tf_op jit(solution)/shard_map/psum | solution.py:72
  868.0 0.8 select_multiply_fusion.2
  868.9 2.5 scatter_fusion
  871.4 1.9 broadcast_multiply_fusion
  873.3 0.8 copy-done.6
  874.1 10.3 fusion.8
  884.5 1.8 multiply_reduce_fusion
  886.4 1.6 gather_fusion.4
  888.0 711.5 %all-reduce.6.cloned.1.call-done = f32[1536,16]{0,1:T(8,128)} async-done(((f32[1536,16]{0,1:T(8,128)}), f32[1536,16]{0,1:T(8,128)}) %all-reduce.6.cloned.1.call-update) | async-done | bytes 98320 | tf_op jit(solution)/shard_map/psum | solution.py:72
  1599.6 0.8 select_multiply_fusion.1
  1600.4 2.7 scatter_fusion.1
  1603.1 1.3 broadcast_multiply_fusion.1
  1604.4 0.8 copy-done.4
  1605.2 10.3 fusion
  1615.5 3.2 fusion.111
  1619.4 711.3 %all-reduce.8.cloned.1.call-done = f32[1536,16]{0,1:T(8,128)} async-done(((f32[1536,16]{0,1:T(8,128)}), f32[1536,16]{0,1:T(8,128)}) %all-reduce.8.cloned.1.call-update) | async-done | bytes 98320 | tf_op jit(solution)/shard_map/psum | solution.py:72
  2330.7 0.8 select_multiply_fusion
  2331.5 0.9 scatter_fusion.2
  2332.5 4.1 fusion.63
  2336.7 9.1 fusion.60
  2346.2 1.2 multiply_reduce_fusion.4
  2347.4 10.3 collective-permute-done
  2357.7 2.4 fusion.69
  2360.2 0.8 copy.63
  2361.0 0.8 copy.64
  2361.8 9.9 collective-permute-done.2
  2371.7 11.5 psum.31
  (71 shorter events, 11.1 us)
Async XLA Ops:
  7.2 121.1 %copy-start = (bf16[512,1024]{1,0:T(8,128)(2,1)S(1)}, bf16[512,1024]{1,0:T(8,128)(2,1)}, u32[]{:S(2)}) copy-start(bf16[512,1024]{1,0:T(8,128)(2,1)} %param.17) | copy-start | bytes 3145732
  10.0 14.4 copy-start.1
  11.2 52.3 %all-to-all-start = ((bf16[64,24,512]{2,1,0:T(8,128)(2,1)}), bf16[64,24,512]{2,1,0:T(8,128)(2,1)}, u32[]{:S(2)}, u32[]{:S(2)}) async-start(bf16[64,24,512]{2,1,0:T(8,128)(2,1)} %stack.6), calls=%async_computation | async-start | bytes 3145728 | tf_op jit(solution)/shard_map/all_to_all | solution.py:14
  25.0 47.9 %copy-start.3 = (bf16[512,512]{1,0:T(8,128)(2,1)S(1)}, bf16[512,512]{1,0:T(8,128)(2,1)}, u32[]{:S(2)}) copy-start(bf16[512,512]{1,0:T(8,128)(2,1)} %param.16) | copy-start | bytes 1572868
  25.0 48.0 %copy-start.8 = (f32[1024,16]{0,1:T(8,128)S(1)}, f32[1024,16]{0,1:T(8,128)}, u32[]{:S(2)}) copy-start(f32[1024,16]{0,1:T(8,128)} %param.13) | copy-start | bytes 196612
  64.7 10.9 copy-start.9
  64.7 11.7 copy-start.11
  64.7 48.1 %all-to-all-start.1 = ((bf16[64,24,512]{2,1,0:T(8,128)(2,1)}), bf16[64,24,512]{2,1,0:T(8,128)(2,1)}, u32[]{:S(2)}, u32[]{:S(2)}) async-start(bf16[64,24,512]{2,1,0:T(8,128)(2,1)} %stack.7), calls=%async_computation.1 | async-start | bytes 3145728 | tf_op jit(solution)/shard_map/all_to_all | solution.py:14
  72.9 1542.6 %collective-permute-start.1 = (bf16[512,512]{1,0:T(8,128)(2,1)S(1)}, bf16[512,512]{1,0:T(8,128)(2,1)}, u32[]{:S(2)}, u32[]{:S(2)}) collective-permute-start(bf16[512,512]{1,0:T(8,128)(2,1)S(1)} %copy-done.3), channel_id=1, source_target_pairs={{0,4},{4,8},{8,12},{12,16},{16,20},{20,24},{24,28},{28,32},{32,36}... | collective-permute-start | bytes 1572872 | tf_op jit(solution)/shard_map/ppermute | solution.py:20
  77.6 44.9 %copy-start.13 = (s32[3,64]{1,0:T(4,128)S(1)}, s32[3,64]{1,0:T(4,128)}, u32[]{:S(2)}) copy-start(s32[3,64]{1,0:T(4,128)} %param.15) | copy-start | bytes 2308
  114.1 48.0 %all-to-all-start.2 = ((bf16[64,24,512]{2,1,0:T(8,128)(2,1)}), bf16[64,24,512]{2,1,0:T(8,128)(2,1)}, u32[]{:S(2)}, u32[]{:S(2)}) async-start(bf16[64,24,512]{2,1,0:T(8,128)(2,1)} %stack.8), calls=%async_computation.2 | async-start | bytes 3145728 | tf_op jit(solution)/shard_map/all_to_all | solution.py:14
  122.2 745.8 %all-reduce.4.cloned.1.call-start = ((), (), s32[]{:S(2)}) async-start(), calls=%async_computation.3 | async-start | bytes 196608 | tf_op jit(solution)/shard_map/psum | solution.py:72
  142.9 1456.7 %all-reduce.6.cloned.1.call-start = ((), (), s32[]{:S(2)}) async-start(), calls=%async_computation.4 | async-start | bytes 196608 | tf_op jit(solution)/shard_map/psum | solution.py:72
  873.3 0.8 copy-start.6
  884.4 1446.2 %all-reduce.8.cloned.1.call-start = ((), (), s32[]{:S(2)}) async-start(), calls=%async_computation.5 | async-start | bytes 196608 | tf_op jit(solution)/shard_map/psum | solution.py:72
  1604.4 0.8 copy-start.4
  1615.5 3.2 copy-start.5
  2332.5 4.2 copy-start.2
  2332.5 4.2 copy-start.10
  2332.5 4.2 copy-start.12
  2336.7 21.0 copy-start.7
  2345.9 11.9 collective-permute-start
  2360.1 11.6 collective-permute-start.2
Sparse Core Ops, SparseCore 0:
  143.0 724.9 all-reduce.3
  884.6 714.9 all-reduce.5
  1615.6 714.9 all-reduce.7
